TPU v7x, 128 devices: a whole 4x4x4 slice. The times are simulated.
128 devices in a mesh: dp: 4 (over y_hi, core), head: 4 (over x), ctx: 8 (over z, y_lo).
Axes of the slice: x: 4, y: 4 (y_hi: 2, y_lo: 2; y = y_hi * 2 + y_lo), z: 4, core: 2. Of those that a mesh axis runs over, the one named last changes fastest.
Arguments:
- video: bfloat16 [16, 64, 24576], P('dp', 'head', 'ctx'), parts along dimension 0, may hold values from -6 to 6
- cache: bfloat16 [8, 64, 24576], P('dp', 'head', 'ctx'), parts along dimension 0, may hold values from -6 to 6
- conv_weight: bfloat16 [3, 3, 288, 192], replicated, may hold values from -0.125 to 0.125
- conv_bias: float32 [192], replicated, may hold values from -3 to 3
- down_weight: bfloat16 [768, 192], replicated, may hold values from -0.21875 to 0.21875
- patch_weight: bfloat16 [768, 5120], P(None, ('head', 'ctx')), may hold values from -0.21875 to 0.21875
- step_index: int32 [4], P('dp'), parts along dimension 0, may hold values from 0 to 999
- mod_weight: bfloat16 [256, 10240], P(None, ('head', 'ctx')), may hold values from -1 to 1
- qkv_weight: bfloat16 [5120, 20, 3, 128], P('ctx', 'head'), may hold values from -0.078125 to 0.078125
Outputs:
- attended: bfloat16 [16384, 2560], P(('dp', 'ctx'), 'head'), parts along dimension 0
There are 4 independent parts, one for each index of `dp`. A program takes and returns all parts, laid end to end along the dimension named above; an argument that names none is the same for every part. Nothing has to cross between parts.
All inputs are finite; a program needn't handle non-finite values.
Results may differ from a plain program's by a relative error of at most 0.015.
The roundings to bfloat16 on the way count: a program that leaves them out, or rounds other values in their place, can miss the bound.
Values may be sent and summed in bfloat16 or wider, within the bound.
No kernel may reach another device: no remote copies, remote signals or barrier semaphores. Data moves between devices by JAX's collectives and lax.ppermute only.
A program may use at most 128 MiB of HBM per device.

v0:
```python
import jax
import jax.numpy as jnp
from jax import lax
from jax.sharding import PartitionSpec as P

D = 5120
HDIM = 128
FREQ = 256


def with_halo(cells, sides, width):
    for axis, dim in sides:
        count = lax.axis_size(axis)
        ends = count - 1
        head = lax.slice_in_dim(cells, 0, width, axis=dim)
        tail = lax.slice_in_dim(cells, cells.shape[dim] - width, cells.shape[dim], axis=dim)
        cells = jnp.concatenate(
            [
                lax.ppermute(tail, axis, [(i, (i + 1) % count) for i in range(ends)]),
                cells,
                lax.ppermute(head, axis, [((i + 1) % count, i) for i in range(ends)]),
            ],
            axis=dim,
        )
    return cells


def silu_act(value):
    return value * jax.nn.sigmoid(value)


def shards(
    video,
    cache,
    conv_weight,
    conv_bias,
    down_weight,
    patch_weight,
    step_index,
    mod_weight,
    qkv_weight,
):
    cin = conv_weight.shape[2] // 3
    cmid = conv_weight.shape[3]
    frame_count = video.shape[0]
    tile_rows = video.shape[1]
    tile_cols = video.shape[2] // cin
    frames = jnp.concatenate([cache, video], 0).reshape(frame_count + 2, tile_rows, tile_cols, cin)
    padded = with_halo(frames, (("head", 1), ("ctx", 2)), 1)
    total = jnp.zeros((frame_count, tile_rows, tile_cols, cmid), jnp.float32)
    for time_tap in range(3):
        for row_tap in range(3):
            slab = padded[time_tap : time_tap + frame_count, row_tap : row_tap + tile_rows]
            stacked = jnp.concatenate(
                [slab[:, :, col_tap : col_tap + tile_cols] for col_tap in range(3)], -1
            )
            total = total + jnp.einsum(
                "fyxc,cd->fyxd",
                stacked,
                conv_weight[time_tap, row_tap],
                preferred_element_type=jnp.float32,
            )
    hidden = silu_act(total + conv_bias).astype(jnp.bfloat16)
    stacked = (
        hidden.reshape(frame_count, tile_rows // 2, 2, tile_cols // 2, 2, cmid)
        .transpose(0, 1, 3, 2, 4, 5)
        .reshape(-1, 4 * cmid)
    )
    reduced = silu_act(jnp.dot(stacked, down_weight, preferred_element_type=jnp.float32)).astype(
        jnp.bfloat16
    )
    reduced = reduced.reshape(frame_count, tile_rows // 2, tile_cols // 2, cmid)
    patches = reduced.reshape(frame_count, tile_rows // 4, 2, tile_cols // 4, 2, cmid).transpose(
        0, 1, 3, 2, 4, 5
    )
    patches = patches.reshape(-1, 4 * cmid)
    half = FREQ // 2
    freqs = jnp.exp(-jnp.log(10000.0) * jnp.arange(half, dtype=jnp.float32) / half)
    angles = step_index[0].astype(jnp.float32) * freqs
    timing = jnp.concatenate([jnp.cos(angles), jnp.sin(angles)]).astype(jnp.bfloat16)
    mod_share = jnp.dot(timing[None, :], mod_weight, preferred_element_type=jnp.float32)[0]
    modulation = lax.all_gather(mod_share, ("head", "ctx"), axis=0, tiled=True)
    scale = modulation[:D]
    shift = modulation[D:]
    embedded = jnp.dot(
        patches,
        lax.all_gather(patch_weight, ("head", "ctx"), axis=1, tiled=True),
        preferred_element_type=jnp.float32,
    )
    inverse = lax.rsqrt(jnp.mean(embedded * embedded, -1, keepdims=True) + 1e-06)
    normed = (embedded * inverse * (1.0 + scale) + shift).astype(jnp.bfloat16)
    gathered = lax.all_gather(normed, "head", axis=0, tiled=True)
    group_rows = gathered.shape[0]
    heads_here = qkv_weight.shape[1]
    out_cols = heads_here * 3 * HDIM
    piece = lax.all_gather(qkv_weight, "ctx", axis=0, tiled=True)
    qkv = jnp.dot(
        gathered, piece.reshape(piece.shape[0], out_cols), preferred_element_type=jnp.float32
    )
    qkv = qkv.astype(jnp.bfloat16).reshape(group_rows, heads_here, 3, HDIM)
    query = qkv[:, :, 0]
    keys = qkv[:, :, 1]
    values = qkv[:, :, 2]
    inv_root = 1.0 / jnp.sqrt(jnp.float32(HDIM))
    best = jnp.full((heads_here, group_rows), -1e30, jnp.float32)
    key_piece = lax.all_gather(keys, "ctx", axis=0, tiled=True)
    value_piece = lax.all_gather(values, "ctx", axis=0, tiled=True)
    scores = (
        jnp.einsum("qhd,khd->hqk", query, key_piece, preferred_element_type=jnp.float32) * inv_root
    )
    new_best = jnp.maximum(best, jnp.max(scores, -1))
    probs = jnp.exp(scores - new_best[..., None])
    denom = jnp.sum(probs, -1)
    accum = jnp.einsum(
        "hqk,khd->hqd", probs.astype(jnp.bfloat16), value_piece, preferred_element_type=jnp.float32
    )
    best, denom, accum = (new_best, denom, accum)
    result = (accum / denom[..., None]).astype(jnp.bfloat16)
    return result.transpose(1, 0, 2).reshape(group_rows, heads_here * HDIM)


def solution(mesh):
    return jax.shard_map(
        shards,
        mesh=mesh,
        in_specs=(
            P("dp", "head", "ctx"),
            P("dp", "head", "ctx"),
            P(),
            P(),
            P(),
            P(None, ("head", "ctx")),
            P("dp"),
            P(None, ("head", "ctx")),
            P("ctx", "head", None, None),
        ),
        out_specs=P(("dp", "ctx"), "head"),
        check_vma=False,
    )
```

profile of v0, /device:TPU:1, one launch (start us, length us, event | category | flops | bytes accessed | tf_op | source)
XLA Modules:
  0.0 923.7 jit_solution(17581543572212077937)
XLA Ops:
  10.8 4.6 collective-permute-start
  15.3 1.3 collective-permute-start.1
  19.2 141.1 %all-reduce = f32[10240]{0:T(1024)S(1)} all-reduce(f32[10240]{0:T(1024)S(1)} %dynamic-update-slice), channel_id=1, replica_groups=mesh['dp'=4,'head'=4,'ctx'=8] {'head','ctx'}, use_global_device_ids=true, to_apply=%add | all-reduce | flops 10240 | bytes 81920
  164.3 1.3 collective-permute-start.2
  165.6 1.5 collective-permute-start.3
  167.6 1.4 collective-permute-done.2
  168.9 1.9 fusion.81
  170.8 1.3 collective-permute-done.3
  172.1 2.1 fusion.73
  181.5 2.6 multiply_convert_fusion
  187.7 8.9 all-gather.8.cloned.1.call-done
  196.7 5.9 multiply_reduce_fusion.1
  202.6 1.5 add_convert_fusion
  204.8 3.1 copy.17
  208.0 63.2 %all-gather.10.cloned.1.call-done = bf16[512,5120]{1,0:T(8,128)(2,1)} async-done(((bf16[128,5120]{1,0:T(8,128)(2,1)}), bf16[512,5120]{1,0:T(8,128)(2,1)}) %all-gather.10.cloned.1.call-update) | async-done | bytes 5242896 | tf_op jit(solution)/shard_map/all_gather | solution.py:92
  271.2 381.9 %all-gather.12.cloned.1.call-done = bf16[5120,5,3,128]{0,3,2,1:T(8,128)(2,1)} async-done(((bf16[640,5,3,128]{0,3,2,1:T(8,128)(2,1)}), bf16[5120,5,3,128]{0,3,2,1:T(8,128)(2,1)}) %all-gather.12.cloned.1.call-update) | async-done | bytes 19660816 | tf_op jit(solution)/shard_map/all_gather | solution.py:96
  653.1 17.7 %convolution_convert_fusion = bf16[512,1920]{1,0:T(8,128)(2,1)} fusion(bf16[512,5120]{1,0:T(8,128)(2,1)} %all-gather.10.cloned.1.call-done, bf16[5120,1920]{0,1:T(8,128)(2,1)} %bitcast.113), kind=kOutput, calls=%fused_computation.24 | convolution fusion | flops 10067312640 | bytes 26869760 | tf_op jit(solution)/shard_map/dot_general | solution.py:97
  670.8 2.7 copy.18
  674.5 1.1 copy.33
  676.2 110.6 %all-gather.14.cloned.1.call-done = bf16[4096,5,1,128]{3,0,1,2:T(8,128)(2,1)} async-done(((bf16[512,5,1,128]{3,0,1,2:T(8,128)(2,1)}), bf16[4096,5,1,128]{3,0,1,2:T(8,128)(2,1)}) %all-gather.14.cloned.1.call-update) | async-done | bytes 5242896 | tf_op jit(solution)/shard_map/all_gather | solution.py:106
  786.8 19.0 %multiply_reduce_fusion = (f32[5,512]{1,0:T(8,128)S(1)}, f32[5,512,4096]{2,1,0:T(8,128)}) fusion(bf16[4096,5,1,128]{3,0,1,2:T(8,128)(2,1)} %all-gather.14.cloned.1.call-done, bf16[512,5,3,128]{0,3,2,1:T(8,128)(2,1)S(1)} %bitcast.108), kind=kOutput, calls=%fused_computation.1 | convolution fusion | flops 2705323520 | bytes 47851520 | tf_op jit(solution)/shard_map/qhd,khd->hqk/dot_general | solution.py:109
  805.8 17.3 %fusion = f32[5,512]{1,0:T(8,128)S(1)} fusion(f32[5,512,4096]{2,1,0:T(8,128)} %get-tuple-element.47, f32[5,512]{1,0:T(8,128)S(1)} %broadcast_maximum_fusion), kind=kLoop, calls=%fused_computation.2 | loop fusion | flops 31454720 | bytes 41963520 | tf_op jit(solution)/shard_map/reduce_sum | solution.py:113
  823.2 75.6 %all-gather.16.cloned.1.call-done = bf16[4096,5,1,128]{0,3,1,2:T(8,128)(2,1)} async-done(((bf16[512,5,1,128]{0,3,1,2:T(8,128)(2,1)}), bf16[4096,5,1,128]{0,3,1,2:T(8,128)(2,1)}) %all-gather.16.cloned.1.call-update) | async-done | bytes 5242896 | tf_op jit(solution)/shard_map/all_gather | solution.py:107
  898.7 17.3 %divide_convert_fusion = bf16[512,5,128]{0,2,1:T(8,128)(2,1)S(1)} fusion(bf16[4096,5,1,128]{0,3,1,2:T(8,128)(2,1)} %all-gather.16.cloned.1.call-done, f32[5,512,4096]{2,1,0:T(8,128)} %get-tuple-element.47, f32[5,512]{1,0:T(8,128)S(1)} %broadcast_maximum_fusion, f32[512,5]{0,1:T(8,128)S(1)} %bitcast.112), kind=kOutput, calls=%fused_computation.84 | convolution fusion | flops 2716467200 | bytes 47861760 | tf_op jit(solution)/shard_map/hqk,khd->hqd/dot_general | solution.py:114
  (70 shorter events, 23.9 us)
Async XLA Ops:
  6.5 180.0 %copy-start = (bf16[768,192]{0,1:T(8,128)(2,1)S(1)}, bf16[768,192]{0,1:T(8,128)(2,1)}, u32[]{:S(2)}) copy-start(bf16[768,192]{0,1:T(8,128)(2,1)} %param.13) | copy-start | bytes 884740
  6.5 10.8 %copy-start.7 = (u32[128]{0:T(128)S(1)}, u32[128]{0:T(128)}, u32[]{:S(2)}) copy-start(u32[128]{0:T(128)} %constant.27) | copy-start | bytes 1540
  6.5 12.2 %copy-start.4 = (bf16[256,320]{0,1:T(8,128)(2,1)S(1)}, bf16[256,320]{0,1:T(8,128)(2,1)}, u32[]{:S(2)}) copy-start(bf16[256,320]{0,1:T(8,128)(2,1)} %param.16) | copy-start | bytes 491524
  6.5 190.1 %all-gather.8.cloned.1.call-start = ((), (), s32[]{:S(2)}) async-start(), calls=%async_computation | async-start | bytes 8110080 | tf_op jit(solution)/shard_map/all_gather | solution.py:87
  7.3 264.0 %all-gather.10.cloned.1.call-start = ((), (), s32[]{:S(2)}) async-start(), calls=%async_computation.1 | async-start | bytes 6553600 | tf_op jit(solution)/shard_map/all_gather | solution.py:92
  8.3 152.2 %copy-start.3 = (bf16[4,16,3072]{2,1,0:T(8,128)(2,1)S(1)}, bf16[4,16,3072]{2,1,0:T(8,128)(2,1)}, u32[]{:S(2)}) copy-start(bf16[4,16,3072]{2,1,0:T(8,128)(2,1)} %param.9) | copy-start | bytes 1179652
  10.8 151.3 %collective-permute-start = (bf16[6,1,32,96]{3,2,1,0:T(8,128)(2,1)}, bf16[6,1,32,96]{3,2,1,0:T(8,128)(2,1)}, u32[]{:S(2)}, u32[]{:S(2)}) collective-permute-start(bf16[6,1,32,96]{3,2,1,0:T(8,128)(2,1)} %get-tuple-element.35), channel_id=1, source_target_pairs={{0,8},{8,16},{16,24},{1,9},{9,17},{17,25},{2,10},{10,18},{18,26},{... | collective-permute-start | bytes 110600 | tf_op jit(solution)/shard_map/ppermute | solution.py:19
  15.3 148.0 %collective-permute-start.1 = (bf16[6,1,32,96]{3,2,1,0:T(8,128)(2,1)}, bf16[6,1,32,96]{3,2,1,0:T(8,128)(2,1)}, u32[]{:S(2)}, u32[]{:S(2)}) collective-permute-start(bf16[6,1,32,96]{3,2,1,0:T(8,128)(2,1)} %get-tuple-element.34), channel_id=1, source_target_pairs={{8,0},{16,8},{24,16},{9,1},{17,9},{25,17},{10,2},{18,10},{26,18},{... | collective-permute-start | bytes 110600 | tf_op jit(solution)/shard_map/ppermute | solution.py:21
  164.3 4.6 collective-permute-start.2
  165.6 6.5 collective-permute-start.3
  170.8 3.4 copy-start.5
  180.5 0.9 copy-start.6
  202.6 2.2 copy-start.2
  204.1 449.0 %all-gather.12.cloned.1.call-start = ((), (), s32[]{:S(2)}) async-start(), calls=%async_computation.2 | async-start | bytes 22118400 | tf_op jit(solution)/shard_map/all_gather | solution.py:96
  207.9 578.8 %all-gather.14.cloned.1.call-start = ((), (), s32[]{:S(2)}) async-start(), calls=%async_computation.3 | async-start | bytes 5898240 | tf_op jit(solution)/shard_map/all_gather | solution.py:106
  675.6 223.2 %all-gather.16.cloned.1.call-start = ((), (), s32[]{:S(2)}) async-start(), calls=%async_computation.4 | async-start | bytes 5898240 | tf_op jit(solution)/shard_map/all_gather | solution.py:107
  898.7 18.4 %copy-start.1 = (bf16[768,192]{0,1:T(8,128)(2,1)S(1)}, bf16[768,192]{0,1:T(8,128)(2,1)}, u32[]{:S(2)}) copy-start(bf16[768,192]{0,1:T(8,128)(2,1)} %param.13) | copy-start | bytes 884740
Sparse Core Ops, SparseCore 0:
  9.0 187.6 all-gather.7
  204.2 66.9 all-gather.9
  272.9 380.1 all-gather.11
  675.7 111.0 all-gather.13
  788.3 110.4 all-gather.15
where the time goes:
time: 924 us
  waiting for transfers between devices  644 us (70%)
  blocking collectives  141 us (15%)
  matrix products  70.4 us (8%)
  other arithmetic  22.9 us (2%)
  local copies, waits for them, and re-layouts  21.4 us (2%)
  between operations  14.9 us (2%)
    all_gather x1, waiting for transfers between devices, shards(): piece = lax.all_gather(qkv_weight, 'ctx', axis=0, tiled=True)  382 us
    unnamed x1, blocking collectives  141 us
    all_gather x1, waiting for transfers between devices, shards(): key_piece = lax.all_gather(keys, 'ctx', axis=0, tiled=True)  111 us
    all_gather x1, waiting for transfers between devices, shards(): value_piece = lax.all_gather(values, 'ctx', axis=0, tiled=True)  75.6 us
    all_gather x1, waiting for transfers between devices, shards(): gathered = lax.all_gather(normed, 'head', axis=0, tiled=True)  63.2 us
    dot_general x1, matrix products, shards(): jnp.einsum('qhd,khd->hqk', query, key_piece, preferred_element_type=jnp.f...  19 us
  transfers between devices with their start and end apart: 9, of which 7 were waited for; matrix products, arithmetic and copies ran while one was open for 7% of the time, Pallas kernels for 0%

commit v1 on v0

--- a/solution.py
+++ b/solution.py
@@ -103,7 +103,10 @@
     values = qkv[:, :, 2]
     inv_root = 1.0 / jnp.sqrt(jnp.float32(HDIM))
     best = jnp.full((heads_here, group_rows), -1e30, jnp.float32)
-    key_piece = lax.all_gather(keys, "ctx", axis=0, tiled=True)
+    oldest = jax.lax.axis_size("ctx")
+    arr_now = jnp.stack([keys] * oldest)
+    block_now = jax.lax.all_to_all(arr_now, "ctx", 0, 0)
+    key_piece = jnp.concatenate(block_now, axis=0)
     value_piece = lax.all_gather(values, "ctx", axis=0, tiled=True)
     scores = (
         jnp.einsum("qhd,khd->hqk", query, key_piece, preferred_element_type=jnp.float32) * inv_root

time: 924 us -> 868 us (0.939)
  waiting for transfers between devices: 644 us -> 466 us
  blocking collectives: 141 us -> 258 us
    all_to_all x0 -> x1, blocking collectives: none -> 118 us  [shards(): block_now = jax.lax.all_to_all(arr_now, 'ctx', 0, 0)]
    all_gather x1 -> x0, waiting for transfers between devices: 111 us -> none  [shards(): key_piece = lax.all_gather(keys, 'ctx', axis=0, tiled=True)]
    all_gather x1, waiting for transfers between devices: 75.6 us -> 5.96 us  [shards(): value_piece = lax.all_gather(values, 'ctx', axis=0, tiled=True)]
  transfers between devices with their start and end apart: 9 -> 8, of which waited for: 7 -> 6; matrix products, arithmetic and copies ran while one was open for 7% -> 8% of each run, Pallas kernels for 0% -> 0%
where the time goes in v1:
time: 868 us; the launch traced here: 867 us
  waiting for transfers between devices  466 us (54%)
  blocking collectives  258 us (30%)
  matrix products  70.5 us (8%)
  local copies, waits for them, and re-layouts  26.2 us (3%)
  other arithmetic  22.8 us (3%)
  between operations  14.8 us (2%)
  starting transfers between devices  8.72 us (1%)
    all_gather x1, waiting for transfers between devices, shards(): piece = lax.all_gather(qkv_weight, 'ctx', axis=0, tiled=True)  382 us
    unnamed x1, blocking collectives  140 us
    all_to_all x1, blocking collectives, shards(): block_now = jax.lax.all_to_all(arr_now, 'ctx', 0, 0)  118 us
    all_gather x1, waiting for transfers between devices, shards(): gathered = lax.all_gather(normed, 'head', axis=0, tiled=True)  64.5 us
    dot_general x1, matrix products, shards(): jnp.einsum('qhd,khd->hqk', query, key_piece, preferred_element_type=jnp.f...  19 us
    dot_general x1, matrix products, shards(): jnp.dot(gathered, piece.reshape(piece.shape[0], out_cols), preferred_elem...  17.7 us
    dot_general x1, matrix products, shards(): jnp.einsum('hqk,khd->hqd', probs.astype(jnp.bfloat16), value_piece, prefe...  17.4 us
  transfers between devices with their start and end apart: 8, of which 6 were waited for; matrix products, arithmetic and copies ran while one was open for 8% of the time, Pallas kernels for 0%

profile of v1, /device:TPU:1, one launch (start us, length us, event | category | flops | bytes accessed | tf_op | source)
XLA Modules:
  0.0 867.4 jit_solution(3521215572100933920)
XLA Ops:
  10.8 4.6 collective-permute-start
  15.3 1.3 collective-permute-start.1
  19.0 139.9 %all-reduce = f32[10240]{0:T(1024)S(1)} all-reduce(f32[10240]{0:T(1024)S(1)} %dynamic-update-slice), channel_id=1, replica_groups=mesh['dp'=4,'head'=4,'ctx'=8] {'head','ctx'}, use_global_device_ids=true, to_apply=%add | all-reduce | flops 10240 | bytes 81920
  162.9 1.3 collective-permute-start.2
  164.2 1.5 collective-permute-start.3
  166.2 1.5 collective-permute-done.2
  167.6 1.9 fusion.80
  170.7 2.1 fusion.72
  180.1 2.6 multiply_convert_fusion
  186.3 10.4 %all-gather.6.cloned.1.call-done = bf16[768,5120]{0,1:T(8,128)(2,1)} async-done(((bf16[768,160]{0,1:T(8,128)(2,1)}), bf16[768,5120]{0,1:T(8,128)(2,1)}) %all-gather.6.cloned.1.call-update) | async-done | bytes 7864336 | tf_op jit(solution)/shard_map/all_gather | solution.py:87
  196.7 5.9 multiply_reduce_fusion.1
  202.7 1.5 add_convert_fusion
  204.9 3.1 copy.26
  208.1 64.5 %all-gather.8.cloned.1.call-done = bf16[512,5120]{1,0:T(8,128)(2,1)} async-done(((bf16[128,5120]{1,0:T(8,128)(2,1)}), bf16[512,5120]{1,0:T(8,128)(2,1)}) %all-gather.8.cloned.1.call-update) | async-done | bytes 5242896 | tf_op jit(solution)/shard_map/all_gather | solution.py:92
  272.5 381.9 %all-gather.10.cloned.1.call-done = bf16[5120,5,3,128]{0,3,2,1:T(8,128)(2,1)} async-done(((bf16[640,5,3,128]{0,3,2,1:T(8,128)(2,1)}), bf16[5120,5,3,128]{0,3,2,1:T(8,128)(2,1)}) %all-gather.10.cloned.1.call-update) | async-done | bytes 19660816 | tf_op jit(solution)/shard_map/all_gather | solution.py:96
  654.4 17.7 %convolution_convert_fusion = bf16[512,1920]{1,0:T(8,128)(2,1)} fusion(bf16[512,5120]{1,0:T(8,128)(2,1)} %all-gather.8.cloned.1.call-done, bf16[5120,1920]{0,1:T(8,128)(2,1)} %bitcast.113), kind=kOutput, calls=%fused_computation.22 | convolution fusion | flops 10067312640 | bytes 26869760 | tf_op jit(solution)/shard_map/dot_general | solution.py:97
  672.2 2.7 copy.27
  676.9 2.3 stack.3
  679.2 118.3 %all_to_all.5 = bf16[8,512,5,128]{3,1,2,0:T(8,128)(2,1)S(1)} all-to-all(bf16[8,512,5,128]{3,1,2,0:T(8,128)(2,1)S(1)} %stack.3), channel_id=1, replica_groups=mesh['dp'=4,'head'=4,'ctx'=8] {'ctx'}, dimensions={0} | all-to-all | bytes 10485760 | tf_op jit(solution)/shard_map/all_to_all | solution.py:108
  797.5 2.6 copy.30
  800.1 19.0 %multiply_reduce_fusion = (f32[5,512]{1,0:T(8,128)S(1)}, f32[5,512,4096]{2,1,0:T(8,128)}) fusion(bf16[4096,5,128]{2,0,1:T(8,128)(2,1)} %bitcast.105, bf16[512,5,3,128]{0,3,2,1:T(8,128)(2,1)S(1)} %bitcast.107), kind=kOutput, calls=%fused_computation.1 | convolution fusion | flops 2705323520 | bytes 47851520 | tf_op jit(solution)/shard_map/qhd,khd->hqk/dot_general | solution.py:112
  819.1 17.3 %fusion = f32[5,512]{1,0:T(8,128)S(1)} fusion(f32[5,512,4096]{2,1,0:T(8,128)} %get-tuple-element.47, f32[5,512]{1,0:T(8,128)S(1)} %broadcast_maximum_fusion), kind=kLoop, calls=%fused_computation.2 | loop fusion | flops 31454720 | bytes 41963520 | tf_op jit(solution)/shard_map/reduce_sum | solution.py:116
  836.4 6.0 all-gather.12.cloned.1.call-done
  842.4 17.4 %divide_convert_fusion = bf16[512,5,128]{0,2,1:T(8,128)(2,1)S(1)} fusion(bf16[4096,5,1,128]{0,3,1,2:T(8,128)(2,1)} %all-gather.12.cloned.1.call-done, f32[5,512,4096]{2,1,0:T(8,128)} %get-tuple-element.47, f32[5,512]{1,0:T(8,128)S(1)} %broadcast_maximum_fusion, f32[512,5]{0,1:T(8,128)S(1)} %bitcast.112), kind=kOutput, calls=%fused_computation.82 | convolution fusion | flops 2716467200 | bytes 47861760 | tf_op jit(solution)/shard_map/hqk,khd->hqd/dot_general | solution.py:117
  (70 shorter events, 25.5 us)
Async XLA Ops:
  6.5 178.6 %copy-start = (bf16[768,192]{0,1:T(8,128)(2,1)S(1)}, bf16[768,192]{0,1:T(8,128)(2,1)}, u32[]{:S(2)}) copy-start(bf16[768,192]{0,1:T(8,128)(2,1)} %param.13) | copy-start | bytes 884740
  6.5 10.8 %copy-start.7 = (u32[128]{0:T(128)S(1)}, u32[128]{0:T(128)}, u32[]{:S(2)}) copy-start(u32[128]{0:T(128)} %constant.27) | copy-start | bytes 1540
  6.5 12.0 %copy-start.4 = (bf16[256,320]{0,1:T(8,128)(2,1)S(1)}, bf16[256,320]{0,1:T(8,128)(2,1)}, u32[]{:S(2)}) copy-start(bf16[256,320]{0,1:T(8,128)(2,1)} %param.16) | copy-start | bytes 491524
  6.5 190.2 %all-gather.6.cloned.1.call-start = ((), (), s32[]{:S(2)}) async-start(), calls=%async_computation.1 | async-start | bytes 8110080 | tf_op jit(solution)/shard_map/all_gather | solution.py:87
  7.3 265.3 %all-gather.8.cloned.1.call-start = ((), (), s32[]{:S(2)}) async-start(), calls=%async_computation.2 | async-start | bytes 6553600 | tf_op jit(solution)/shard_map/all_gather | solution.py:92
  8.3 150.8 %copy-start.3 = (bf16[4,16,3072]{2,1,0:T(8,128)(2,1)S(1)}, bf16[4,16,3072]{2,1,0:T(8,128)(2,1)}, u32[]{:S(2)}) copy-start(bf16[4,16,3072]{2,1,0:T(8,128)(2,1)} %param.9) | copy-start | bytes 1179652
  10.8 149.9 %collective-permute-start = (bf16[6,1,32,96]{3,2,1,0:T(8,128)(2,1)}, bf16[6,1,32,96]{3,2,1,0:T(8,128)(2,1)}, u32[]{:S(2)}, u32[]{:S(2)}) collective-permute-start(bf16[6,1,32,96]{3,2,1,0:T(8,128)(2,1)} %get-tuple-element.35), channel_id=1, source_target_pairs={{0,8},{8,16},{16,24},{1,9},{9,17},{17,25},{2,10},{10,18},{18,26},{... | collective-permute-start | bytes 110600 | tf_op jit(solution)/shard_map/ppermute | solution.py:19
  15.3 146.6 %collective-permute-start.1 = (bf16[6,1,32,96]{3,2,1,0:T(8,128)(2,1)}, bf16[6,1,32,96]{3,2,1,0:T(8,128)(2,1)}, u32[]{:S(2)}, u32[]{:S(2)}) collective-permute-start(bf16[6,1,32,96]{3,2,1,0:T(8,128)(2,1)} %get-tuple-element.34), channel_id=1, source_target_pairs={{8,0},{16,8},{24,16},{9,1},{17,9},{25,17},{10,2},{18,10},{26,18},{... | collective-permute-start | bytes 110600 | tf_op jit(solution)/shard_map/ppermute | solution.py:21
  162.9 4.7 collective-permute-start.2
  164.2 6.5 collective-permute-start.3
  169.5 3.4 copy-start.5
  179.2 0.9 copy-start.6
  202.7 2.2 copy-start.2
  204.2 450.2 %all-gather.10.cloned.1.call-start = ((), (), s32[]{:S(2)}) async-start(), calls=%async_computation.3 | async-start | bytes 22118400 | tf_op jit(solution)/shard_map/all_gather | solution.py:96
  208.0 634.4 %all-gather.12.cloned.1.call-start = ((), (), s32[]{:S(2)}) async-start(), calls=%async_computation.4 | async-start | bytes 5898240 | tf_op jit(solution)/shard_map/all_gather | solution.py:110
  842.4 18.5 %copy-start.1 = (bf16[768,192]{0,1:T(8,128)(2,1)S(1)}, bf16[768,192]{0,1:T(8,128)(2,1)}, u32[]{:S(2)}) copy-start(bf16[768,192]{0,1:T(8,128)(2,1)} %param.13) | copy-start | bytes 884740
Sparse Core Ops, SparseCore 0:
  9.0 187.6 all-gather.5
  204.3 68.1 all-gather.7
  274.2 380.1 all-gather.9
  676.0 166.3 all-gather.11
